TPU v7x, 512 devices: a whole 4x4x16 slice. The times are simulated.
512 devices in a mesh: req: 128 (over x, z, core), head: 4 (over y).
Axes of the slice: x: 4, y: 4, z: 16, core: 2. Of those that a mesh axis runs over, the one named last changes fastest.
Arguments:
- queries: bfloat16 [128, 16, 2048], P('req', None, 'head'), may hold values from -6 to 6
- forget_logits: bfloat16 [128, 16, 2048], P('req', None, 'head'), may hold values from -8 to 8
- values: bfloat16 [128, 16, 2048], P('req', None, 'head'), may hold values from -6 to 6
- gate_input: bfloat16 [128, 16, 2048], P('req', None, 'head'), may hold values from -6 to 6
- init_states: float32 [128, 16, 128, 128], P('req', 'head'), may hold values from -4 to 4
- norm_gain: float32 [128], replicated, may hold values from 0.1 to 1.9
- out_weight: bfloat16 [2048, 2048], P('head'), may hold values from -0.125 to 0.125
- dealing: int32 [128], P('req'), may hold values from 0 to 127, as said below
- accepted: int32 [128], P('req'), may hold values from 0 to 16, as said below
Outputs:
- verified: bfloat16 [128, 16, 2048], P('req', None, 'head')
- new_states: float32 [128, 16, 128, 128], P('req', 'head')
Inputs may be any that keep to these rules, and one draw needn't show every extreme that they name: `dealing`: each request appears in exactly one dealt slot. `accepted`: some request accepts all 16 draft tokens and some accepts none.
All inputs are finite; a program needn't handle non-finite values.
Results may differ from a plain program's by a relative error of at most 0.0049.
Values may be sent and summed in bfloat16 or wider, within the bound.
No kernel may reach another device: no remote copies, remote signals or barrier semaphores. Data moves between devices by JAX's collectives and lax.ppermute only.
A program may use at most 64 MiB of HBM per device.

v0:
```python
import jax
import jax.numpy as jnp
from jax import lax
from jax.sharding import PartitionSpec as P

lower_bound = 0.8
norm_eps = 1e-05


def route_gathered(token_tuple, deal_all, worker, local_count):
    mine = worker * local_count + jnp.arange(local_count, dtype=jnp.int32)
    shard_rows = (
        lax.all_gather(token_tuple[0], "req", axis=0, tiled=True),
        lax.all_gather(token_tuple[1], "req", axis=0, tiled=True),
        lax.all_gather(token_tuple[2], "req", axis=0, tiled=True),
        lax.all_gather(token_tuple[3], "req", axis=0, tiled=True),
    )
    match = (deal_all[None, :] == mine[:, None]).astype(jnp.bfloat16)
    totals = tuple(
        (
            jnp.einsum("rk,kte->rte", match, rows, preferred_element_type=jnp.float32)
            for rows in shard_rows
        )
    )
    return tuple((acc.astype(jnp.bfloat16) for acc in totals))


def per_device(
    queries,
    forget_logits,
    values,
    gate_input,
    init_states,
    norm_gain,
    out_weight,
    dealing,
    accepted,
):
    local_count = queries.shape[0]
    draft_len = queries.shape[1]
    head_local = init_states.shape[1]
    head_size = init_states.shape[3]
    deal_all = lax.all_gather(dealing, "req", axis=0, tiled=True)
    worker = lax.axis_index("req")
    token_tuple = (queries, forget_logits, values, gate_input)
    tokens_q, tokens_f, tokens_v, tokens_g = route_gathered(
        token_tuple, deal_all, worker, local_count
    )

    def heads_of(tensor):
        return jnp.moveaxis(
            tensor.astype(jnp.float32).reshape(local_count, draft_len, head_local, head_size), 1, 0
        )

    query_seq = heads_of(tokens_q)
    forget_seq = lower_bound + (1.0 - lower_bound) * jax.nn.sigmoid(heads_of(tokens_f))
    value_seq = heads_of(tokens_v)
    numbers = jnp.arange(1, draft_len + 1, dtype=jnp.int32)

    def advance(state_pair, inputs):
        current, chosen = state_pair
        query_now, forget_now, value_now, number = inputs
        current = (
            forget_now[..., None] * current
            + (1.0 - forget_now)[..., None] * value_now[..., None, :]
        )
        chosen = jnp.where((accepted == number)[:, None, None, None], current, chosen)
        output = jnp.einsum("rhk,rhkv->rhv", query_now, current, precision=lax.Precision.HIGHEST)
        return ((current, chosen), output)

    (last_state, new_states), outputs = lax.scan(
        advance, (init_states, init_states), (query_seq, forget_seq, value_seq, numbers)
    )
    outputs = jnp.moveaxis(outputs, 0, 1)
    meansq = jnp.mean(outputs * outputs, axis=-1, keepdims=True)
    gate_heads = tokens_g.astype(jnp.float32).reshape(local_count, draft_len, head_local, head_size)
    mixed_rows = (
        outputs * lax.rsqrt(meansq + norm_eps) * norm_gain * jax.nn.silu(gate_heads)
    ).astype(jnp.bfloat16)
    mixed_rows = mixed_rows.reshape(local_count * draft_len, head_local * head_size)
    partial_out = jnp.dot(mixed_rows, out_weight, preferred_element_type=jnp.float32)
    summed = lax.psum_scatter(partial_out, "head", scatter_dimension=1, tiled=True)
    verified = summed.astype(jnp.bfloat16).reshape(local_count, draft_len, summed.shape[1])
    return (verified, new_states)


def solution(mesh):
    placed = (
        P("req", None, "head"),
        P("req", None, "head"),
        P("req", None, "head"),
        P("req", None, "head"),
        P("req", "head", None, None),
        P(),
        P("head", None),
        P("req"),
        P("req"),
    )
    return jax.shard_map(
        per_device,
        mesh=mesh,
        in_specs=placed,
        out_specs=(P("req", None, "head"), P("req", "head", None, None)),
        check_vma=False,
    )
```

profile of v0, /device:TPU:2, one launch (start us, length us, event | category | flops | bytes accessed | tf_op | source)
XLA Modules:
  0.0 614.6 jit_solution(16999576388277183235)
XLA Ops:
  7.2 1.1 copy.69
  8.4 0.7 all-gather.9.cloned.1.call-update
  9.1 0.7 all-gather.5.cloned.1.call-update
  11.1 1.3 dynamic-slice
  12.4 0.8 dynamic-update-slice
  13.2 33.1 %all-reduce = s32[128]{0:T(128)S(1)} all-reduce(s32[128]{0:T(128)S(1)} %dynamic-update-slice), channel_id=1, replica_groups=mesh['req'=128,'head'=4] {'req'}, use_global_device_ids=true, to_apply=%add | all-reduce | flops 128 | bytes 1024
  46.3 0.7 broadcast_bitcast_fusion
  46.9 108.4 %all-gather.7.cloned.1.call-done = bf16[128,16,512]{2,1,0:T(8,128)(2,1)} async-done(((bf16[1,16,512]{2,1,0:T(8,128)(2,1)}), bf16[128,16,512]{2,1,0:T(8,128)(2,1)}) %all-gather.7.cloned.1.call-update) | async-done | bytes 2097168 | tf_op jit(solution)/shard_map/all_gather | solution.py:15
  155.3 3.9 fusion.6
  159.2 136.3 %all-gather.9.cloned.1.call-done = bf16[128,16,512]{2,1,0:T(8,128)(2,1)} async-done(((bf16[1,16,512]{2,1,0:T(8,128)(2,1)}), bf16[128,16,512]{2,1,0:T(8,128)(2,1)}) %all-gather.9.cloned.1.call-update) | async-done | bytes 2097168 | tf_op jit(solution)/shard_map/all_gather | solution.py:13
  295.5 3.9 fusion.4
  299.4 136.3 %all-gather.5.cloned.1.call-done = bf16[128,16,512]{2,1,0:T(8,128)(2,1)} async-done(((bf16[1,16,512]{2,1,0:T(8,128)(2,1)}), bf16[128,16,512]{2,1,0:T(8,128)(2,1)}) %all-gather.5.cloned.1.call-update) | async-done | bytes 2097168 | tf_op jit(solution)/shard_map/all_gather | solution.py:14
  435.7 3.9 fusion.8
  439.7 40.8 %while.14 = (s32[]{:T(128)}, f32[1,4,128,128]{3,2,1,0:T(8,128)S(1)}, f32[1,4,128,128]{3,2,1,0:T(8,128)S(1)}, f32[16,1,4,128]{3,2,1,0:T(4,128)S(1)}, f32[16,1,4,1...) while((s32[]{:T(128)}, ...), condition=%wide.region_1.2_spmd, body=%wide.region_0.1_spmd.sunk | while | flops 1049091 | bytes 1339531 | solution.py:71
  439.7 0.6 dynamic_slice.23
  444.8 0.6 dynamic_slice.23
  449.9 0.6 dynamic_slice.23
  457.5 0.6 dynamic_slice.23
  462.6 0.6 dynamic_slice.23
  480.6 95.3 %all-gather.11.cloned.1.call-done = bf16[128,16,512]{2,1,0:T(8,128)(2,1)} async-done(((bf16[1,16,512]{2,1,0:T(8,128)(2,1)}), bf16[128,16,512]{2,1,0:T(8,128)(2,1)}) %all-gather.11.cloned.1.call-update) | async-done | bytes 2097168 | tf_op jit(solution)/shard_map/all_gather | solution.py:16
  575.9 3.9 fusion.2
  579.8 1.0 fusion.16
  580.9 25.8 %reduce-scatter.2.cloned.1.call-done = f32[16,512]{1,0:T(8,128)} async-done(((f32[16,2048]{1,0:T(8,128)}), f32[16,512]{1,0:T(8,128)}) %reduce-scatter.2.cloned.1.call-update) | async-done | bytes 32784 | tf_op jit(solution)/shard_map/reduce_scatter | solution.py:82
  606.7 1.4 convert_bitcast_fusion
  (132 shorter events, 17.6 us)
Async XLA Ops:
  7.2 572.6 %copy-start = (bf16[512,2048]{1,0:T(8,128)(2,1)S(1)}, bf16[512,2048]{1,0:T(8,128)(2,1)}, u32[]{:S(2)}) copy-start(bf16[512,2048]{1,0:T(8,128)(2,1)} %param.17) | copy-start | bytes 6291460
  7.2 148.1 %all-gather.7.cloned.1.call-start = ((), (), s32[]{:S(2)}) async-start(), calls=%async_computation.2 | async-start | bytes 2113536 | tf_op jit(solution)/shard_map/all_gather | solution.py:15
  8.3 287.2 %all-gather.9.cloned.1.call-start = ((), (), s32[]{:S(2)}) async-start(), calls=%async_computation.3 | async-start | bytes 2113536 | tf_op jit(solution)/shard_map/all_gather | solution.py:13
  9.1 426.6 %all-gather.5.cloned.1.call-start = ((), (), s32[]{:S(2)}) async-start(), calls=%async_computation.1 | async-start | bytes 2113536 | tf_op jit(solution)/shard_map/all_gather | solution.py:14
  9.8 566.0 %all-gather.11.cloned.1.call-start = ((), (), s32[]{:S(2)}) async-start(), calls=%async_computation.4 | async-start | bytes 2113536 | tf_op jit(solution)/shard_map/all_gather | solution.py:16
  10.4 596.3 %reduce-scatter.2.cloned.1.call-start = ((), (), s32[]{:S(2)}) async-start(), calls=%async_computation.5 | async-start | bytes 163840 | tf_op jit(solution)/shard_map/reduce_scatter | solution.py:82
  480.4 100.4 %copy-start.1 = (f32[1,4,128,128]{3,2,1,0:T(8,128)}, f32[1,4,128,128]{3,2,1,0:T(8,128)S(1)}, u32[]{:S(2)}) copy-start(f32[1,4,128,128]{3,2,1,0:T(8,128)S(1)} %get-tuple-element.49) | copy-start | bytes 786436
Sparse Core Ops, SparseCore 0:
  11.1 144.1 all-gather.6
  158.4 137.0 all-gather.8
  298.7 137.0 all-gather.4
  438.7 137.0 all-gather.10
  581.0 25.6 reduce-scatter.1
where the time goes:
time: 615 us
  waiting for transfers between devices  504 us (82%)
  blocking collectives  33.1 us (5%)
  matrix products  21.6 us (4%)
  loops' own time  21.3 us (3%)
  between operations  14.5 us (2%)
  local copies, waits for them, and re-layouts  13.8 us (2%)
    all_gather x1, waiting for transfers between devices, route_gathered(): lax.all_gather(token_tuple[1], 'req', axis=0, tiled=True)  136 us
    all_gather x1, waiting for transfers between devices, route_gathered(): lax.all_gather(token_tuple[0], 'req', axis=0, tiled=True)  136 us
    all_gather x1, waiting for transfers between devices, route_gathered(): lax.all_gather(token_tuple[2], 'req', axis=0, tiled=True)  108 us
    all_gather x1, waiting for transfers between devices, route_gathered(): lax.all_gather(token_tuple[3], 'req', axis=0, tiled=True)  95.3 us
    unnamed x1, blocking collectives  33.1 us
    reduce_scatter x1, waiting for transfers between devices, per_device(): lax.psum_scatter(partial_out, 'head', scatter_dimension=1, tiled=True)  25.8 us
    another operation x1, loops' own time, per_device(): lax.scan(advance, (init_states, init_states), (query_seq, forget_seq, val...  21.3 us
    dot_general x4, matrix products, route_gathered(): jnp.einsum('rk,kte->rte', match, rows, preferred_element_type=jnp.float32)  15.5 us
  transfers between devices with their start and end apart: 5, of which 5 were waited for; matrix products, arithmetic and copies ran while one was open for 6% of the time, Pallas kernels for 0%

commit v1 on v0

--- a/solution.py
+++ b/solution.py
@@ -1,3 +1,4 @@
+import functools
 import jax
 import jax.numpy as jnp
 from jax import lax
@@ -7,12 +8,22 @@
 norm_eps = 1e-05
 
 
+def floor_shape(body, which_axis, dimension_no):
+    reached = jnp.stack([body for _ in range(jax.lax.psum(1, which_axis))])
+    everything = jax.lax.all_to_all(reached, which_axis, 0, 0)
+    f_now = jnp.concatenate(everything, axis=dimension_no)
+    return f_now
+
+
+_answer_state = functools.partial(floor_shape, which_axis="req", dimension_no=0)
+
+
 def route_gathered(token_tuple, deal_all, worker, local_count):
     mine = worker * local_count + jnp.arange(local_count, dtype=jnp.int32)
     shard_rows = (
         lax.all_gather(token_tuple[0], "req", axis=0, tiled=True),
         lax.all_gather(token_tuple[1], "req", axis=0, tiled=True),
-        lax.all_gather(token_tuple[2], "req", axis=0, tiled=True),
+        _answer_state(token_tuple[2]),
         lax.all_gather(token_tuple[3], "req", axis=0, tiled=True),
     )
     match = (deal_all[None, :] == mine[:, None]).astype(jnp.bfloat16)

time: 615 us -> 526 us (0.86)
  waiting for transfers between devices: 504 us -> 314 us
  blocking collectives: 33.1 us -> 112 us
  starting transfers between devices: 0.19 us -> 20.3 us
    all_gather x1, waiting for transfers between devices: 136 us -> 14 us  [route_gathered(): lax.all_gather(token_tuple[0], 'req', axis=0, tiled=True)]
    all_gather x1 -> x0, waiting for transfers between devices: 108 us -> none  [route_gathered(): lax.all_gather(token_tuple[2], 'req', axis=0, tiled=True)]
    unnamed x1, blocking collectives: 33.1 us -> 112 us
    all_gather x1, waiting for transfers between devices: 95.3 us -> 136 us  [route_gathered(): lax.all_gather(token_tuple[3], 'req', axis=0, tiled=True)]
    all_to_all x0 -> x1, starting transfers between devices: none -> 20.1 us  [floor_shape(): everything = jax.lax.all_to_all(reached, which_axis, 0, 0)]
  transfers between devices with their start and end apart: 5 -> 5, of which waited for: 5 -> 4; matrix products, arithmetic and copies ran while one was open for 6% -> 3% of each run, Pallas kernels for 0% -> 0%
where the time goes in v1:
time: 526 us; the launch traced here: 525 us
  waiting for transfers between devices  314 us (60%)
  blocking collectives  112 us (21%)
  matrix products  21.6 us (4%)
  loops' own time  21.3 us (4%)
  starting transfers between devices  20.3 us (4%)
  local copies, waits for them, and re-layouts  15.5 us (3%)
  between operations  14.5 us (3%)
  other arithmetic  6.03 us (1%)
    all_gather x1, waiting for transfers between devices, route_gathered(): lax.all_gather(token_tuple[3], 'req', axis=0, tiled=True)  136 us
    all_gather x1, waiting for transfers between devices, route_gathered(): lax.all_gather(token_tuple[1], 'req', axis=0, tiled=True)  136 us
    unnamed x1, blocking collectives  112 us
    reduce_scatter x1, waiting for transfers between devices, per_device(): lax.psum_scatter(partial_out, 'head', scatter_dimension=1, tiled=True)  25.8 us
    another operation x1, loops' own time, per_device(): lax.scan(advance, (init_states, init_states), (query_seq, forget_seq, val...  21.3 us
    all_to_all x1, starting transfers between devices, floor_shape(): everything = jax.lax.all_to_all(reached, which_axis, 0, 0)  20.1 us
    dot_general x4, matrix products, route_gathered(): jnp.einsum('rk,kte->rte', match, rows, preferred_element_type=jnp.float32)  15.5 us
    all_gather x1, waiting for transfers between devices, route_gathered(): lax.all_gather(token_tuple[0], 'req', axis=0, tiled=True)  14 us
  transfers between devices with their start and end apart: 5, of which 4 were waited for; matrix products, arithmetic and copies ran while one was open for 3% of the time, Pallas kernels for 0%

profile of v1, /device:TPU:2, one launch (start us, length us, event | category | flops | bytes accessed | tf_op | source)
XLA Modules:
  0.0 525.1 jit_solution(15153452044687888120)
XLA Ops:
  7.2 1.1 copy.69
  8.4 0.7 all-gather.4.cloned.1.call-update
  9.1 2.3 stack.2
  11.4 20.1 %all-to-all-start = ((bf16[128,1,16,512]{3,2,1,0:T(8,128)(2,1)}), bf16[128,1,16,512]{3,2,1,0:T(8,128)(2,1)}, u32[]{:S(2)}, u32[]{:S(2)}) async-start(bf16[128,1,16,512]{3,2,1,0:T(8,128)(2,1)} %stack.2), calls=%async_computation | async-start | bytes 4194304 | tf_op jit(solution)/shard_map/all_to_all | solution.py:13
  31.6 0.7 all-gather.8.cloned.1.call-update
  33.0 1.3 dynamic-slice
  34.3 0.8 dynamic-update-slice
  35.0 112.1 %all-reduce = s32[128]{0:T(128)S(1)} all-reduce(s32[128]{0:T(128)S(1)} %dynamic-update-slice), channel_id=1, replica_groups=mesh['req'=128,'head'=4] {'req'}, use_global_device_ids=true, to_apply=%add | all-reduce | flops 128 | bytes 1024
  147.2 14.0 %all-gather.6.cloned.1.call-done = bf16[128,16,512]{2,1,0:T(8,128)(2,1)} async-done(((bf16[1,16,512]{2,1,0:T(8,128)(2,1)}), bf16[128,16,512]{2,1,0:T(8,128)(2,1)}) %all-gather.6.cloned.1.call-update) | async-done | bytes 2097168 | tf_op jit(solution)/shard_map/all_gather | solution.py:24
  161.2 3.9 fusion.4
  165.1 136.1 %all-gather.4.cloned.1.call-done = bf16[128,16,512]{2,1,0:T(8,128)(2,1)} async-done(((bf16[1,16,512]{2,1,0:T(8,128)(2,1)}), bf16[128,16,512]{2,1,0:T(8,128)(2,1)}) %all-gather.4.cloned.1.call-update) | async-done | bytes 2097168 | tf_op jit(solution)/shard_map/all_gather | solution.py:25
  301.3 3.9 fusion.8
  305.2 136.3 %all-gather.8.cloned.1.call-done = bf16[128,16,512]{2,1,0:T(8,128)(2,1)} async-done(((bf16[1,16,512]{2,1,0:T(8,128)(2,1)}), bf16[128,16,512]{2,1,0:T(8,128)(2,1)}) %all-gather.8.cloned.1.call-update) | async-done | bytes 2097168 | tf_op jit(solution)/shard_map/all_gather | solution.py:27
  441.5 3.9 fusion.2
  445.4 3.9 fusion.6
  449.3 40.8 %while.14 = (s32[]{:T(128)}, f32[1,4,128,128]{3,2,1,0:T(8,128)S(1)}, f32[1,4,128,128]{3,2,1,0:T(8,128)S(1)}, f32[16,1,4,128]{3,2,1,0:T(4,128)S(1)}, f32[16,1,4,1...) while((s32[]{:T(128)}, ...), condition=%wide.region_1.2_spmd, body=%wide.region_0.1_spmd.sunk | while | flops 1049091 | bytes 1339531 | solution.py:82
  451.8 0.6 dynamic_slice.23
  456.9 0.6 dynamic_slice.23
  462.0 0.6 dynamic_slice.23
  469.7 0.6 dynamic_slice.23
  474.8 0.6 dynamic_slice.23
  490.3 1.0 fusion.16
  491.3 25.8 %reduce-scatter.2.cloned.1.call-done = f32[16,512]{1,0:T(8,128)} async-done(((f32[16,2048]{1,0:T(8,128)}), f32[16,512]{1,0:T(8,128)}) %reduce-scatter.2.cloned.1.call-update) | async-done | bytes 32784 | tf_op jit(solution)/shard_map/reduce_scatter | solution.py:93
  517.2 1.4 convert_bitcast_fusion
  (134 shorter events, 17.1 us)
Async XLA Ops:
  7.2 483.1 %copy-start = (bf16[512,2048]{1,0:T(8,128)(2,1)S(1)}, bf16[512,2048]{1,0:T(8,128)(2,1)}, u32[]{:S(2)}) copy-start(bf16[512,2048]{1,0:T(8,128)(2,1)} %param.17) | copy-start | bytes 6291460
  7.2 154.0 %all-gather.6.cloned.1.call-start = ((), (), s32[]{:S(2)}) async-start(), calls=%async_computation.3 | async-start | bytes 2113536 | tf_op jit(solution)/shard_map/all_gather | solution.py:24
  8.3 292.9 %all-gather.4.cloned.1.call-start = ((), (), s32[]{:S(2)}) async-start(), calls=%async_computation.2 | async-start | bytes 2113536 | tf_op jit(solution)/shard_map/all_gather | solution.py:25
  11.4 135.8 %copy-start.2 = (f32[128]{0:T(128)S(1)}, f32[128]{0:T(128)}, u32[]{:S(2)}) copy-start(f32[128]{0:T(128)} %param.16) | copy-start | bytes 1540
  11.4 434.0 %all-to-all-start = ((bf16[128,1,16,512]{3,2,1,0:T(8,128)(2,1)}), bf16[128,1,16,512]{3,2,1,0:T(8,128)(2,1)}, u32[]{:S(2)}, u32[]{:S(2)}) async-start(bf16[128,1,16,512]{3,2,1,0:T(8,128)(2,1)} %stack.2), calls=%async_computation | async-start | bytes 4194304 | tf_op jit(solution)/shard_map/all_to_all | solution.py:13
  31.5 410.0 %all-gather.8.cloned.1.call-start = ((), (), s32[]{:S(2)}) async-start(), calls=%async_computation.4 | async-start | bytes 2113536 | tf_op jit(solution)/shard_map/all_gather | solution.py:27
  32.3 484.9 %reduce-scatter.2.cloned.1.call-start = ((), (), s32[]{:S(2)}) async-start(), calls=%async_computation.5 | async-start | bytes 163840 | tf_op jit(solution)/shard_map/reduce_scatter | solution.py:93
  490.1 28.5 %copy-start.1 = (f32[1,4,128,128]{3,2,1,0:T(8,128)}, f32[1,4,128,128]{3,2,1,0:T(8,128)S(1)}, u32[]{:S(2)}) copy-start(f32[1,4,128,128]{3,2,1,0:T(8,128)S(1)} %get-tuple-element.49) | copy-start | bytes 786436
Sparse Core Ops, SparseCore 0:
  11.1 150.0 all-gather.5
  164.4 136.8 all-gather.3
  304.4 137.0 all-gather.7
  491.4 25.6 reduce-scatter.1
